TPU v7x, 512 devices: a whole 4x8x8 slice. The times are simulated.
512 devices in a mesh: dp: 32 (over z, x), fsdp: 16 (over y, core).
Axes of the slice: x: 4, y: 8, z: 8, core: 2. Of those that a mesh axis runs over, the one named last changes fastest.
Arguments:
- projected: bfloat16 [65536, 2304], P(('dp', 'fsdp')), may hold values from -7.03125 to 7.03125
- out_weight: bfloat16 [768, 1536], P('fsdp'), may hold values from -0.21875 to 0.21875
- kernel: float32 [31, 1536], replicated, may hold values from -2 to 2
- cotangent: bfloat16 [65536, 1536], P(('dp', 'fsdp')), may hold values from -6 to 6
- send_rows: int32 [65536], P(('dp', 'fsdp')), may hold values from -1 to 127, as said below
- compute_src: int32 [65536], P(('dp', 'fsdp')), may hold values from -1 to 127, as said below
- segment: int32 [65536], P(('dp', 'fsdp')), may hold values from -1 to 3, as said below
Outputs:
- block_out: bfloat16 [65536, 1536], P(('dp', 'fsdp'))
- projected_grad: bfloat16 [65536, 2304], P(('dp', 'fsdp'))
- out_weight_grad: float32 [768, 1536], P('fsdp')
- kernel_grad: float32 [31, 1536], replicated
Inputs may be any that keep to these rules, and one draw needn't show every extreme that they name: `send_rows`: A device's 128 entries are 32 blocks of 4, block t for index t of dp at the same fsdp index; each lists rows of the device's own block of projected, each row at most once, filled entries first in a block and -1 after them. In every draw some device of each fsdp index fills all its entries. `compute_src`: on device (t, f), a row holds s * 4 + k when it receives entry t * 4 + k of device (s, f); every filled entry of send_rows is received by exactly one row, and a row holds -1 when it receives nothing. Filled rows come first. In every draw some device of each fsdp index receives a full block from every device. On each device, rows with compute_src = -1 hold -1, the others hold segment numbers from 0 that never fall along the rows.
All inputs are finite; a program needn't handle non-finite values.
Results may differ from a plain program's by a relative error of at most 0.018.
Values may be sent and summed in bfloat16 or wider, within the bound.
No kernel may reach another device: no remote copies, remote signals or barrier semaphores. Data moves between devices by JAX's collectives and lax.ppermute only.
A program may use at most 128 MiB of HBM per device.

v0:
```python
import jax
import jax.numpy as jnp
from jax import lax
from jax.sharding import Mesh, PartitionSpec as P

DP = ("dz", "dx")
FSDP = ("fy", "fc")
HEADS = 8
HEAD_DIM = 96


def split_heads(frames):
    length = frames.shape[0]
    inner_width = HEADS * HEAD_DIM
    query_part = frames[:, :inner_width].reshape(length, HEADS, HEAD_DIM)
    key_part = frames[:, inner_width : 2 * inner_width].reshape(length, HEADS, HEAD_DIM)
    value_part = frames[:, 2 * inner_width :].reshape(length, HEADS, HEAD_DIM)
    return (query_part, key_part, value_part)


def attend(frames, segment):
    query_part, key_part, value_part = split_heads(frames)
    scores = jnp.einsum(
        "qhd,khd->hqk", query_part, key_part, preferred_element_type=jnp.float32
    ) * HEAD_DIM ** (-0.5)
    inside = segment[:, None] == segment[None, :]
    scores = jnp.where(inside[None], scores, -1e30)
    highest = jnp.max(scores, axis=2, keepdims=True)
    weights = jnp.exp(scores - highest)
    soft_probs = weights / jnp.sum(weights, axis=2, keepdims=True)
    rounded = soft_probs.astype(jnp.bfloat16)
    context = jnp.einsum("hqk,khd->qhd", rounded, value_part, preferred_element_type=jnp.float32)
    return (
        context.reshape(frames.shape[0], HEADS * HEAD_DIM).astype(jnp.bfloat16),
        soft_probs,
        rounded,
    )


def attend_back(frames, soft_probs, rounded, context_grad):
    query_part, key_part, value_part = split_heads(frames)
    length = frames.shape[0]
    inner_width = HEADS * HEAD_DIM
    upstream = context_grad.reshape(length, HEADS, HEAD_DIM)
    value_grad = jnp.einsum("hqk,qhd->khd", rounded, upstream, preferred_element_type=jnp.float32)
    prob_grad = jnp.einsum("qhd,khd->hqk", upstream, value_part, preferred_element_type=jnp.float32)
    score_grad = soft_probs * (prob_grad - jnp.sum(prob_grad * soft_probs, axis=2, keepdims=True))
    score_grad = (score_grad * HEAD_DIM ** (-0.5)).astype(jnp.bfloat16)
    query_grad = jnp.einsum(
        "hqk,khd->qhd", score_grad, key_part, preferred_element_type=jnp.float32
    )
    key_grad = jnp.einsum(
        "hqk,qhd->khd", score_grad, query_part, preferred_element_type=jnp.float32
    )
    return jnp.concatenate(
        [
            query_grad.reshape(length, inner_width).astype(jnp.bfloat16),
            key_grad.reshape(length, inner_width).astype(jnp.bfloat16),
            value_grad.reshape(length, inner_width).astype(jnp.bfloat16),
        ],
        axis=1,
    )


def finish(mixed, kernel, segment):
    length = mixed.shape[0]
    tap_count = kernel.shape[0]
    half_span = (tap_count - 1) // 2
    signal = mixed.astype(jnp.float32)
    padded = jnp.pad(signal, ((half_span, half_span), (0, 0)))
    neighbours = jnp.pad(segment, (half_span, half_span), constant_values=-2)
    convolved = jnp.zeros_like(signal)
    for offset in range(tap_count):
        matching = (neighbours[offset : offset + length] == segment).astype(jnp.float32)
        convolved = (
            convolved + kernel[offset] * padded[offset : offset + length] * matching[:, None]
        )
    return signal + jax.nn.silu(convolved)


def body(projected, out_weight, kernel, cotangent, send_rows, compute_src, segment):
    row_count = projected.shape[0]
    present = send_rows >= 0
    outgoing = jnp.take(projected, jnp.maximum(send_rows, 0), axis=0)
    outgoing = jnp.where(present[:, None], outgoing, jnp.zeros_like(outgoing))
    incoming = lax.all_to_all(outgoing, DP, split_axis=0, concat_axis=0, tiled=True)
    filled = compute_src >= 0
    frames = jnp.take(incoming, jnp.maximum(compute_src, 0), axis=0)
    frames = jnp.where(filled[:, None], frames, jnp.zeros_like(frames))
    context, soft_probs, rounded = attend(frames, segment)
    columns = context
    mixed_sums = jnp.dot(
        columns,
        lax.all_gather(out_weight, FSDP, axis=0, tiled=True),
        preferred_element_type=jnp.float32,
    )
    mixed = mixed_sums.astype(jnp.bfloat16)
    result, pullback = jax.vjp(
        lambda signal, kernel_taps: finish(signal, kernel_taps, segment), mixed, kernel
    )
    mixed_grad, kernel_part = pullback(cotangent.astype(jnp.float32))
    columns = context
    weight_share = lax.psum_scatter(
        jnp.einsum("rc,rd->cd", columns, mixed_grad, preferred_element_type=jnp.float32).astype(
            jnp.bfloat16
        ),
        FSDP,
        scatter_dimension=0,
        tiled=True,
    ).astype(jnp.float32)
    context_grad = jnp.einsum(
        "rd,cd->rc",
        mixed_grad,
        lax.all_gather(out_weight, FSDP, axis=0, tiled=True),
        preferred_element_type=jnp.float32,
    ).astype(jnp.bfloat16)
    frame_grad = attend_back(frames, soft_probs, rounded, context_grad)
    slot_total = incoming.shape[0]
    back_index = jnp.where(filled, compute_src, slot_total)
    returning = jnp.zeros_like(incoming).at[back_index].set(frame_grad, mode="drop")
    arrived = lax.all_to_all(returning, DP, split_axis=0, concat_axis=0, tiled=True)
    source_index = jnp.where(present, send_rows, row_count)
    projected_grad = jnp.zeros_like(projected).at[source_index].set(arrived, mode="drop")
    scale_factor = (row_count * lax.axis_size(DP) * lax.axis_size(FSDP)) ** (-0.5)
    weight_share, arrived = lax.optimization_barrier((weight_share, arrived))
    kernel_piece = sum_rows(kernel_part, FSDP)
    owned_rows = weight_share.shape[0]
    both = jnp.concatenate([weight_share, kernel_piece], axis=0)
    piece = sum_rows(both, DP)
    both = gather_rows(piece, DP)[: both.shape[0]]
    weight_total = both[:owned_rows]
    kernel_total = gather_rows(both[owned_rows:], FSDP)[: kernel.shape[0]]
    return (
        result.astype(jnp.bfloat16),
        projected_grad,
        weight_total * scale_factor,
        kernel_total * scale_factor,
    )


def sum_rows(x, axis):
    count = lax.axis_size(axis)
    per = -(-x.shape[0] // count)
    padded = jnp.pad(x, ((0, count * per - x.shape[0]), (0, 0)))
    got = lax.all_to_all(
        padded.reshape(count, per, x.shape[1]), axis, split_axis=0, concat_axis=0, tiled=True
    )
    return jnp.sum(got, axis=0)


def gather_rows(piece, axis):
    count = lax.axis_size(axis)
    copies = jnp.broadcast_to(piece[None], (count, *piece.shape))
    got = lax.all_to_all(copies, axis, split_axis=0, concat_axis=0, tiled=True)
    return got.reshape(count * piece.shape[0], piece.shape[1])


def solution(mesh):
    dp_count, fsdp_count = mesh.devices.shape
    fine = Mesh(
        mesh.devices.reshape(dp_count // 4, 4, fsdp_count // 2, 2), ("dz", "dx", "fy", "fc")
    )
    placed = (
        P((*DP, *FSDP), None),
        P(FSDP, None),
        P(),
        P((*DP, *FSDP), None),
        P((*DP, *FSDP)),
        P((*DP, *FSDP)),
        P((*DP, *FSDP)),
    )
    return jax.shard_map(
        body,
        mesh=fine,
        in_specs=placed,
        out_specs=(P((*DP, *FSDP), None), P((*DP, *FSDP), None), P(FSDP, None), P()),
        check_vma=False,
    )
```

profile of v0, /device:TPU:1, one launch (start us, length us, event | category | flops | bytes accessed | tf_op | source)
XLA Modules:
  0.0 211.4 jit_solution(173523416918727866)
XLA Ops:
  7.2 0.7 all-gather.2.cloned.1.call-update
  7.9 1.2 compare_select_fusion.1
  9.2 1.0 gather_fusion
  10.2 0.2 select_select_fusion.1
  10.4 1.0 all_to_all.28
  11.3 13.7 %all-to-all-start = ((bf16[32,4,2304]{2,1,0:T(4,128)(2,1)}), bf16[32,4,2304]{2,1,0:T(4,128)(2,1)S(1)}, u32[]{:S(2)}, u32[]{:S(2)}) async-start(bf16[32,4,2304]{2,1,0:T(4,128)(2,1)} %all_to_all.28), calls=%async_computation | async-start | bytes 1179648 | tf_op jit(solution)/shard_map/all_to_all | solution.py:86
  25.1 0.2 slice_reduce_fusion.29
  25.3 0.5 compare_select_fusion
  25.8 0.3 slice_reduce_fusion.30
  26.6 16.0 %all-to-all-done = bf16[32,4,2304]{2,1,0:T(4,128)(2,1)S(1)} async-done(((bf16[32,4,2304]{2,1,0:T(4,128)(2,1)}), bf16[32,4,2304]{2,1,0:T(4,128)(2,1)S(1)}, u32[]{:S(2)}, u32[]{:S(2)}) %all-to-all-start) | async-done | bytes 589856 | tf_op jit(solution)/shard_map/all_to_all | solution.py:86
  42.5 0.1 all_to_all.30
  42.7 1.0 gather_fusion.1
  43.6 0.2 select_select_fusion
  43.8 0.2 copy.47
  44.0 0.2 copy.46
  44.2 0.2 copy.45
  44.3 1.2 fusion.39
  45.5 0.6 copy-done.47
  46.1 0.5 convolution_convert_fusion.6
  46.6 11.6 %all-gather.2.cloned.1.call-done = bf16[768,1536]{1,0:T(8,128)(2,1)} async-done(((bf16[48,1536]{1,0:T(8,128)(2,1)}), bf16[768,1536]{1,0:T(8,128)(2,1)}) %all-gather.2.cloned.1.call-update) | async-done | bytes 2359312 | tf_op jit(solution)/shard_map/all_gather | solution.py:94
  58.2 2.2 %fusion.2 = f32[128,1536]{1,0:T(8,128)S(1)} fusion(bf16[128,768]{0,1:T(8,128)(2,1)S(1)} %bitcast.38, bf16[768,1536]{1,0:T(8,128)(2,1)} %all-gather.2.cloned.1.call-done), kind=kOutput, calls=%fused_computation.8 | convolution fusion | flops 302383104 | bytes 3342336 | tf_op jit(solution)/shard_map/dot_general | solution.py:92
  60.4 7.7 %multiply_reduce_fusion.31 = (f32[1536]{0:T(1024)}, f32[1536]{0:T(1024)}, f32[1536]{0:T(1024)}, f32[1536]{0:T(1024)}, f32[1536]{0:T(1024)}, /*index=5*/f32[1536]...) fusion(f32[128,1536]{1,0:T(8,128)S(1)} %fusion.2, ...), kind=kLoop, calls=%fused_computation.99 | loop fusion | flops 25152000 | bytes 3013632 | tf_op jit(solution)/shard_map/transpose(jvp())/reduce_sum | solution.py:76
  68.2 2.3 %multiply_reduce_fusion.16 = (f32[1536]{0:T(1024)}, f32[1536]{0:T(1024)}, f32[1536]{0:T(1024)}, f32[1536]{0:T(1024)}, f32[1536]{0:T(1024)}, /*index=5*/f32[1536]...) fusion(f32[128,1536]{1,0:T(8,128)S(1)} %get-tuple-element.69, ...), kind=kLoop, calls=%fused_computation.84 | loop fusion | flops 5294592 | bytes 2424832 | tf_op jit(solution)/shard_map/transpose(jvp())/reduce_sum | solution.py:76
  70.4 0.5 multiply_multiply_fusion.27
  71.0 0.7 multiply_multiply_fusion.29
  71.8 0.7 multiply_multiply_fusion.28
  72.5 2.6 %multiply_reduce_fusion.4 = (f32[1536]{0:T(1024)}, f32[1536]{0:T(1024)}, f32[1536]{0:T(1024)}, f32[1536]{0:T(1024)}, f32[128,1536]{1,0:T(8,128)S(1)}, /*index=5*...) fusion(f32[128,1536]{1,0:T(8,128)S(1)} %get-tuple-element.69, ...), kind=kLoop, calls=%fused_computation.72 | loop fusion | flops 5105664 | bytes 7535616 | tf_op jit(solution)/shard_map/transpose(jvp())/reduce_sum | solution.py:76
  75.1 2.6 %pad_add_fusion = f32[158,1536]{1,0:T(8,128)S(1)} fusion(f32[128,1536]{1,0:T(8,128)S(1)} %get-tuple-element.78, f32[128,1536]{1,0:T(8,128)S(1)} %get-tuple-element.80, f32[128,1536]{1,0:T(8,128)S(1)} %get-tuple-element.81, f32[128,1536]{1,0:T(8,128)S(1)} %get-tuple-element.82, f32[128,1536]{1,0:T(8,128)S(1)} %get-tuple-element.83, ...), kind=kLoop, calls=%fused_computation.59 | loop fusion | flops 5824512 | bytes 20631552 | tf_op jit(solution)/shard_map/transpose(jvp())/add_any | solution.py:76
  77.7 0.7 fusion.16
  78.6 2.2 %convolution_convert_fusion = bf16[768,1536]{1,0:T(8,128)(2,1)} fusion(bf16[128,768]{0,1:T(8,128)(2,1)S(1)} %bitcast.39, bf16[128,1536]{1,0:T(8,128)(2,1)S(1)} %fusion.16), kind=kOutput, calls=%fused_computation.6 | convolution fusion | flops 303169536 | bytes 2949120 | tf_op jit(solution)/shard_map/rc,rd->cd/dot_general | solution.py:104
  81.1 2.0 multiply_reduce_fusion.22
  83.6 0.3 pad_add_fusion.7
  83.9 0.8 reshape.309
  84.7 4.6 %all-to-all-start.2 = ((f32[16,2,1536]{2,1,0:T(2,128)}), f32[16,2,1536]{2,1,0:T(2,128)S(1)}, u32[]{:S(2)}, u32[]{:S(2)}) async-start(f32[16,2,1536]{2,1,0:T(2,128)} %reshape.309), calls=%async_computation.3 | async-start | bytes 393216 | tf_op jit(solution)/shard_map/all_to_all | solution.py:145
  89.3 2.5 %convolution_convert_fusion.5 = bf16[128,768]{1,0:T(8,128)(2,1)S(1)} fusion(bf16[128,1536]{1,0:T(8,128)(2,1)S(1)} %fusion.16, bf16[768,1536]{1,0:T(8,128)(2,1)} %all-gather.2.cloned.1.call-done), kind=kOutput, calls=%fused_computation.54 | convolution fusion | flops 302088192 | bytes 2949120 | tf_op jit(solution)/shard_map/rd,cd->rc/dot_general | solution.py:111
  91.9 0.2 copy.49
  92.0 1.3 convolution_convert_fusion.2
  93.3 0.1 copy.55
  93.5 0.3 fusion.40
  93.8 1.6 convolution_convert_fusion.3
  95.4 0.1 copy.54
  95.5 1.6 convolution_convert_fusion.4
  97.1 0.1 copy.53
  97.3 1.8 scatter_custom_fusion
  99.0 1.0 all_to_all.31
  100.0 10.0 %all-to-all-start.1 = ((bf16[32,4,2304]{2,1,0:T(4,128)(2,1)}), bf16[32,4,2304]{2,1,0:T(4,128)(2,1)S(1)}, u32[]{:S(2)}, u32[]{:S(2)}) async-start(bf16[32,4,2304]{2,1,0:T(4,128)(2,1)} %all_to_all.31), calls=%async_computation.1 | async-start | bytes 1179648 | tf_op jit(solution)/shard_map/all_to_all | solution.py:121
  110.1 17.9 %all-to-all-done.1 = bf16[32,4,2304]{2,1,0:T(4,128)(2,1)S(1)} async-done(((bf16[32,4,2304]{2,1,0:T(4,128)(2,1)}), bf16[32,4,2304]{2,1,0:T(4,128)(2,1)S(1)}, u32[]{:S(2)}, u32[]{:S(2)}) %all-to-all-start.1) | async-done | bytes 589856 | tf_op jit(solution)/shard_map/all_to_all | solution.py:121
  128.1 0.1 reshape.340
  128.2 12.4 %reduce-scatter.2.cloned.1.call-done = bf16[48,1536]{1,0:T(8,128)(2,1)} async-done(((bf16[768,1536]{1,0:T(8,128)(2,1)}), bf16[48,1536]{1,0:T(8,128)(2,1)}) %reduce-scatter.2.cloned.1.call-update) | async-done | bytes 147472 | tf_op jit(solution)/shard_map/reduce_scatter | solution.py:103
  140.6 0.9 convert_element_type.216
  141.5 0.2 reshape.310
  141.8 20.6 %all_to_all.44 = f32[32,2,1536]{2,1,0:T(2,128)S(1)} all-to-all(f32[32,2,1536]{2,1,0:T(2,128)S(1)} %reshape.310), channel_id=1, replica_groups=mesh['dz'=8,'dx'=4,'fy'=8,'fc'=2] {'dz','dx'}, dimensions={0} | all-to-all | bytes 786432 | tf_op jit(solution)/shard_map/all_to_all | solution.py:145
  162.3 0.1 reduce_sum.365
  162.5 0.8 broadcast_in_dim.55
  163.3 4.1 %all-to-all-start.4 = ((f32[32,2,1536]{2,1,0:T(2,128)}), f32[32,2,1536]{2,1,0:T(2,128)S(1)}, u32[]{:S(2)}, u32[]{:S(2)}) async-start(f32[32,2,1536]{2,1,0:T(2,128)} %broadcast_in_dim.55), calls=%async_computation.5 | async-start | bytes 786432 | tf_op jit(solution)/shard_map/all_to_all | solution.py:154
  167.4 2.4 %scatter_custom_fusion.1 = bf16[128,2304]{1,0:T(8,128)(2,1)} fusion(s32[128]{0:T(128)} %get-tuple-element.108, bf16[128,2304]{1,0:T(8,128)(2,1)S(1)} %reshape.340, bf16[]{:T(256)} %constant.10.clone.1), kind=kCustom, calls=%fused_computation.145 | custom fusion | bytes 590336 | tf_op jit(solution)/shard_map/scatter | solution.py:123
  169.8 9.1 %all-to-all-done.4 = f32[32,2,1536]{2,1,0:T(2,128)S(1)} async-done(((f32[32,2,1536]{2,1,0:T(2,128)}), f32[32,2,1536]{2,1,0:T(2,128)S(1)}, u32[]{:S(2)}, u32[]{:S(2)}) %all-to-all-start.4) | async-done | bytes 393248 | tf_op jit(solution)/shard_map/all_to_all | solution.py:154
  178.9 0.7 broadcast_in_dim.57
  179.6 13.8 %all-to-all-start.5 = ((f32[16,2,1536]{2,1,0:T(2,128)}), f32[16,2,1536]{2,1,0:T(2,128)S(1)}, u32[]{:S(2)}, u32[]{:S(2)}) async-start(f32[16,2,1536]{2,1,0:T(2,128)} %broadcast_in_dim.57), calls=%async_computation.6 | async-start | bytes 393216 | tf_op jit(solution)/shard_map/all_to_all | solution.py:154
  193.4 0.1 slice_multiply_fusion
  193.6 0.9 mul.1323
  194.5 9.3 %all-to-all-done.5 = f32[16,2,1536]{2,1,0:T(2,128)S(1)} async-done(((f32[16,2,1536]{2,1,0:T(2,128)}), f32[16,2,1536]{2,1,0:T(2,128)S(1)}, u32[]{:S(2)}, u32[]{:S(2)}) %all-to-all-start.5) | async-done | bytes 196640 | tf_op jit(solution)/shard_map/all_to_all | solution.py:154
  203.8 0.1 reshape.311
  203.9 0.7 slice_multiply_fusion.1
  (144 shorter events, 1.0 us)
Async XLA Ops:
  7.2 2.0 copy-start
  7.2 51.1 %all-gather.2.cloned.1.call-start = ((), (), s32[]{:S(2)}) async-start(), calls=%async_computation.7 | async-start | bytes 2506752 | tf_op jit(solution)/shard_map/all_gather | solution.py:94
  9.1 1.0 copy-start.45
  10.1 14.9 %copy-start.4 = (f32[31,1536]{1,0:T(8,128)S(1)}, f32[31,1536]{1,0:T(8,128)}, u32[]{:S(2)}) copy-start(f32[31,1536]{1,0:T(8,128)} %param.11) | copy-start | bytes 571396
  10.2 15.1 %copy-start.46 = (s32[128]{0:T(128)S(1)}, s32[128]{0:T(128)}, u32[]{:S(2)}) copy-start(s32[128]{0:T(128)} %param.14) | copy-start | bytes 1540
  10.2 16.0 %copy-start.44 = (s32[128]{0:T(128)S(1)}, s32[128]{0:T(128)}, u32[]{:S(2)}) copy-start(s32[128]{0:T(128)} %param.15) | copy-start | bytes 1540
  11.3 31.2 %all-to-all-start = ((bf16[32,4,2304]{2,1,0:T(4,128)(2,1)}), bf16[32,4,2304]{2,1,0:T(4,128)(2,1)S(1)}, u32[]{:S(2)}, u32[]{:S(2)}) async-start(bf16[32,4,2304]{2,1,0:T(4,128)(2,1)} %all_to_all.28), calls=%async_computation | async-start | bytes 1179648 | tf_op jit(solution)/shard_map/all_to_all | solution.py:86
  25.0 115.5 %reduce-scatter.2.cloned.1.call-start = ((), (), s32[]{:S(2)}) async-start(), calls=%async_computation.8 | async-start | bytes 2506752 | tf_op jit(solution)/shard_map/reduce_scatter | solution.py:103
  26.4 44.6 %copy-start.38 = (f32[128]{0:T(128)}, f32[128]{0:T(128)S(1)}, u32[]{:S(2)}) copy-start(f32[128]{0:T(128)S(1)} %get-tuple-element.122) | copy-start | bytes 1540
  26.4 44.6 %copy-start.40 = (f32[128]{0:T(128)}, f32[128]{0:T(128)S(1)}, u32[]{:S(2)}) copy-start(f32[128]{0:T(128)S(1)} %get-tuple-element.123) | copy-start | bytes 1540
  26.4 44.6 %copy-start.42 = (f32[128]{0:T(128)}, f32[128]{0:T(128)S(1)}, u32[]{:S(2)}) copy-start(f32[128]{0:T(128)S(1)} %get-tuple-element.124) | copy-start | bytes 1540
  26.4 45.3 %copy-start.26 = (f32[128]{0:T(128)}, f32[128]{0:T(128)S(1)}, u32[]{:S(2)}) copy-start(f32[128]{0:T(128)S(1)} %get-tuple-element.116) | copy-start | bytes 1540
  26.4 45.3 %copy-start.28 = (f32[128]{0:T(128)}, f32[128]{0:T(128)S(1)}, u32[]{:S(2)}) copy-start(f32[128]{0:T(128)S(1)} %get-tuple-element.117) | copy-start | bytes 1540
  26.4 45.3 %copy-start.30 = (f32[128]{0:T(128)}, f32[128]{0:T(128)S(1)}, u32[]{:S(2)}) copy-start(f32[128]{0:T(128)S(1)} %get-tuple-element.118) | copy-start | bytes 1540
  26.4 45.3 %copy-start.32 = (f32[128]{0:T(128)}, f32[128]{0:T(128)S(1)}, u32[]{:S(2)}) copy-start(f32[128]{0:T(128)S(1)} %get-tuple-element.119) | copy-start | bytes 1540
  26.4 45.3 %copy-start.34 = (f32[128]{0:T(128)}, f32[128]{0:T(128)S(1)}, u32[]{:S(2)}) copy-start(f32[128]{0:T(128)S(1)} %get-tuple-element.120) | copy-start | bytes 1540
  26.5 45.3 %copy-start.36 = (f32[128]{0:T(128)}, f32[128]{0:T(128)S(1)}, u32[]{:S(2)}) copy-start(f32[128]{0:T(128)S(1)} %get-tuple-element.121) | copy-start | bytes 1540
  26.6 19.0 %copy-start.25 = (pred[128,128]{0,1:T(8,128)(4,1)}, pred[128,128]{0,1:T(8,128)(4,1)S(1)}, u32[]{:S(2)}) copy-start(pred[128,128]{0,1:T(8,128)(4,1)S(1)} %broadcast_compare_fusion) | copy-start | bytes 49156
  44.2 14.1 %copy-start.2 = (bf16[128,768]{0,1:T(8,128)(2,1)}, bf16[128,768]{0,1:T(8,128)(2,1)S(1)}, u32[]{:S(2)}) copy-start(bf16[128,768]{0,1:T(8,128)(2,1)S(1)} %copy.46) | copy-start | bytes 589828
  45.5 0.6 copy-start.47
  46.6 13.8 %copy-start.1 = (bf16[128,1536]{1,0:T(8,128)(2,1)S(1)}, bf16[128,1536]{1,0:T(8,128)(2,1)}, u32[]{:S(2)}) copy-start(bf16[128,1536]{1,0:T(8,128)(2,1)} %param.12) | copy-start | bytes 1179652
  78.4 2.4 %copy-start.20 = (f32[1536]{0:T(1024)S(1)}, f32[1536]{0:T(1024)}, u32[]{:S(2)}) copy-start(f32[1536]{0:T(1024)} %get-tuple-element.7) | copy-start | bytes 18436
  78.4 2.5 %copy-start.19 = (f32[1536]{0:T(1024)S(1)}, f32[1536]{0:T(1024)}, u32[]{:S(2)}) copy-start(f32[1536]{0:T(1024)} %get-tuple-element.8) | copy-start | bytes 18436
  78.4 2.5 %copy-start.18 = (f32[1536]{0:T(1024)S(1)}, f32[1536]{0:T(1024)}, u32[]{:S(2)}) copy-start(f32[1536]{0:T(1024)} %get-tuple-element.9) | copy-start | bytes 18436
  78.4 2.5 %copy-start.17 = (f32[1536]{0:T(1024)S(1)}, f32[1536]{0:T(1024)}, u32[]{:S(2)}) copy-start(f32[1536]{0:T(1024)} %get-tuple-element.10) | copy-start | bytes 18436
  78.4 2.5 %copy-start.16 = (f32[1536]{0:T(1024)S(1)}, f32[1536]{0:T(1024)}, u32[]{:S(2)}) copy-start(f32[1536]{0:T(1024)} %get-tuple-element.11) | copy-start | bytes 18436
  78.4 2.5 %copy-start.15 = (f32[1536]{0:T(1024)S(1)}, f32[1536]{0:T(1024)}, u32[]{:S(2)}) copy-start(f32[1536]{0:T(1024)} %get-tuple-element.12) | copy-start | bytes 18436
  78.5 2.5 %copy-start.14 = (f32[1536]{0:T(1024)S(1)}, f32[1536]{0:T(1024)}, u32[]{:S(2)}) copy-start(f32[1536]{0:T(1024)} %get-tuple-element.13) | copy-start | bytes 18436
  78.5 2.5 %copy-start.13 = (f32[1536]{0:T(1024)S(1)}, f32[1536]{0:T(1024)}, u32[]{:S(2)}) copy-start(f32[1536]{0:T(1024)} %get-tuple-element.14) | copy-start | bytes 18436
  78.5 2.6 %copy-start.12 = (f32[1536]{0:T(1024)S(1)}, f32[1536]{0:T(1024)}, u32[]{:S(2)}) copy-start(f32[1536]{0:T(1024)} %get-tuple-element.15) | copy-start | bytes 18436
  78.5 2.6 %copy-start.27 = (f32[128]{0:T(128)S(1)}, f32[128]{0:T(128)}, u32[]{:S(2)}) copy-start(f32[128]{0:T(128)} %copy-done.26) | copy-start | bytes 1540
  78.5 2.6 %copy-start.29 = (f32[128]{0:T(128)S(1)}, f32[128]{0:T(128)}, u32[]{:S(2)}) copy-start(f32[128]{0:T(128)} %copy-done.28) | copy-start | bytes 1540
  78.5 2.6 %copy-start.31 = (f32[128]{0:T(128)S(1)}, f32[128]{0:T(128)}, u32[]{:S(2)}) copy-start(f32[128]{0:T(128)} %copy-done.30) | copy-start | bytes 1540
  78.5 2.6 %copy-start.33 = (f32[128]{0:T(128)S(1)}, f32[128]{0:T(128)}, u32[]{:S(2)}) copy-start(f32[128]{0:T(128)} %copy-done.32) | copy-start | bytes 1540
  78.5 2.6 %copy-start.35 = (f32[128]{0:T(128)S(1)}, f32[128]{0:T(128)}, u32[]{:S(2)}) copy-start(f32[128]{0:T(128)} %copy-done.34) | copy-start | bytes 1540
  78.5 2.6 %copy-start.37 = (f32[128]{0:T(128)S(1)}, f32[128]{0:T(128)}, u32[]{:S(2)}) copy-start(f32[128]{0:T(128)} %copy-done.36) | copy-start | bytes 1540
  78.5 2.6 %copy-start.39 = (f32[128]{0:T(128)S(1)}, f32[128]{0:T(128)}, u32[]{:S(2)}) copy-start(f32[128]{0:T(128)} %copy-done.38) | copy-start | bytes 1540
  78.6 2.6 %copy-start.41 = (f32[128]{0:T(128)S(1)}, f32[128]{0:T(128)}, u32[]{:S(2)}) copy-start(f32[128]{0:T(128)} %copy-done.40) | copy-start | bytes 1540
  78.6 2.6 %copy-start.43 = (f32[128]{0:T(128)S(1)}, f32[128]{0:T(128)}, u32[]{:S(2)}) copy-start(f32[128]{0:T(128)} %copy-done.42) | copy-start | bytes 1540
  80.7 2.5 %copy-start.11 = (f32[1536]{0:T(1024)S(1)}, f32[1536]{0:T(1024)}, u32[]{:S(2)}) copy-start(f32[1536]{0:T(1024)} %get-tuple-element.25) | copy-start | bytes 18436
  80.7 2.5 %copy-start.10 = (f32[1536]{0:T(1024)S(1)}, f32[1536]{0:T(1024)}, u32[]{:S(2)}) copy-start(f32[1536]{0:T(1024)} %get-tuple-element.26) | copy-start | bytes 18436
  80.7 2.6 %copy-start.9 = (f32[1536]{0:T(1024)S(1)}, f32[1536]{0:T(1024)}, u32[]{:S(2)}) copy-start(f32[1536]{0:T(1024)} %get-tuple-element.27) | copy-start | bytes 18436
  80.7 2.6 %copy-start.8 = (f32[1536]{0:T(1024)S(1)}, f32[1536]{0:T(1024)}, u32[]{:S(2)}) copy-start(f32[1536]{0:T(1024)} %get-tuple-element.28) | copy-start | bytes 18436
  80.7 2.6 %copy-start.7 = (f32[1536]{0:T(1024)S(1)}, f32[1536]{0:T(1024)}, u32[]{:S(2)}) copy-start(f32[1536]{0:T(1024)} %get-tuple-element.29) | copy-start | bytes 18436
  80.8 2.6 %copy-start.6 = (f32[1536]{0:T(1024)S(1)}, f32[1536]{0:T(1024)}, u32[]{:S(2)}) copy-start(f32[1536]{0:T(1024)} %get-tuple-element.30) | copy-start | bytes 18436
  80.8 2.6 %copy-start.5 = (f32[1536]{0:T(1024)S(1)}, f32[1536]{0:T(1024)}, u32[]{:S(2)}) copy-start(f32[1536]{0:T(1024)} %get-tuple-element.31) | copy-start | bytes 18436
  80.8 2.7 %copy-start.24 = (f32[1536]{0:T(1024)S(1)}, f32[1536]{0:T(1024)}, u32[]{:S(2)}) copy-start(f32[1536]{0:T(1024)} %get-tuple-element.34) | copy-start | bytes 18436
  80.8 2.7 %copy-start.23 = (f32[1536]{0:T(1024)S(1)}, f32[1536]{0:T(1024)}, u32[]{:S(2)}) copy-start(f32[1536]{0:T(1024)} %get-tuple-element.35) | copy-start | bytes 18436
  80.8 2.7 %copy-start.22 = (f32[1536]{0:T(1024)S(1)}, f32[1536]{0:T(1024)}, u32[]{:S(2)}) copy-start(f32[1536]{0:T(1024)} %get-tuple-element.36) | copy-start | bytes 18436
  80.8 2.7 %copy-start.21 = (f32[1536]{0:T(1024)S(1)}, f32[1536]{0:T(1024)}, u32[]{:S(2)}) copy-start(f32[1536]{0:T(1024)} %get-tuple-element.37) | copy-start | bytes 18436
  83.5 8.5 %copy-start.3 = (bf16[128,768]{0,1:T(8,128)(2,1)S(1)}, bf16[128,768]{0,1:T(8,128)(2,1)}, u32[]{:S(2)}) copy-start(bf16[128,768]{0,1:T(8,128)(2,1)} %copy-done.2) | copy-start | bytes 589828
  83.6 8.5 %copy-start.48 = (f32[8,128]{1,0:T(8,128)S(1)}, f32[8,128]{1,0:T(8,128)}, u32[]{:S(2)}) copy-start(f32[8,128]{1,0:T(8,128)} %copy-done.47) | copy-start | bytes 12292
  84.7 15.3 %all-to-all-start.2 = ((f32[16,2,1536]{2,1,0:T(2,128)}), f32[16,2,1536]{2,1,0:T(2,128)S(1)}, u32[]{:S(2)}, u32[]{:S(2)}) async-start(f32[16,2,1536]{2,1,0:T(2,128)} %reshape.309), calls=%async_computation.3 | async-start | bytes 393216 | tf_op jit(solution)/shard_map/all_to_all | solution.py:145
  100.0 28.1 %all-to-all-start.1 = ((bf16[32,4,2304]{2,1,0:T(4,128)(2,1)}), bf16[32,4,2304]{2,1,0:T(4,128)(2,1)S(1)}, u32[]{:S(2)}, u32[]{:S(2)}) async-start(bf16[32,4,2304]{2,1,0:T(4,128)(2,1)} %all_to_all.31), calls=%async_computation.1 | async-start | bytes 1179648 | tf_op jit(solution)/shard_map/all_to_all | solution.py:121
  163.3 15.6 %all-to-all-start.4 = ((f32[32,2,1536]{2,1,0:T(2,128)}), f32[32,2,1536]{2,1,0:T(2,128)S(1)}, u32[]{:S(2)}, u32[]{:S(2)}) async-start(f32[32,2,1536]{2,1,0:T(2,128)} %broadcast_in_dim.55), calls=%async_computation.5 | async-start | bytes 786432 | tf_op jit(solution)/shard_map/all_to_all | solution.py:154
  179.6 24.2 %all-to-all-start.5 = ((f32[16,2,1536]{2,1,0:T(2,128)}), f32[16,2,1536]{2,1,0:T(2,128)S(1)}, u32[]{:S(2)}, u32[]{:S(2)}) async-start(f32[16,2,1536]{2,1,0:T(2,128)} %broadcast_in_dim.57), calls=%async_computation.6 | async-start | bytes 393216 | tf_op jit(solution)/shard_map/all_to_all | solution.py:154
Sparse Core Ops, SparseCore 0:
  10.1 48.0 all-gather.1
  81.0 59.5 reduce-scatter.1
where the time goes:
time: 212 us; the launch traced here: 211 us
  waiting for transfers between devices  76.9 us (36%)
  starting transfers between devices  46.4 us (22%)
  other arithmetic  26.2 us (12%)
  blocking collectives  20.6 us (10%)
  between operations  15.3 us (7%)
  matrix products  13.3 us (6%)
  local copies, waits for them, and re-layouts  12.8 us (6%)
    all_to_all x1, blocking collectives, sum_rows(): lax.all_to_all(padded.reshape(count, per, x.shape[1]), axis, split_axis=0...  20.6 us
    all_to_all x2, waiting for transfers between devices, gather_rows(): got = lax.all_to_all(copies, axis, split_axis=0, concat_axis=0, tiled=True)  18.4 us
    all_to_all x2, starting transfers between devices, gather_rows(): got = lax.all_to_all(copies, axis, split_axis=0, concat_axis=0, tiled=True)  17.9 us
    all_to_all x1, waiting for transfers between devices, body(): lax.all_to_all(returning, DP, split_axis=0, concat_axis=0, tiled=True)  17.9 us
    all_to_all x1, waiting for transfers between devices, body(): lax.all_to_all(outgoing, DP, split_axis=0, concat_axis=0, tiled=True)  16 us
    reduce_sum x4, other arithmetic, finish(): kernel[offset] * padded[offset:offset + length] * matching[:, None]  14.6 us
    all_to_all x1, starting transfers between devices, body(): lax.all_to_all(outgoing, DP, split_axis=0, concat_axis=0, tiled=True)  13.7 us
    reduce_scatter x1, waiting for transfers between devices, body(): lax.psum_scatter(jnp.einsum('rc,rd->cd', columns, mixed_grad, preferred_e...  12.4 us
  transfers between devices with their start and end apart: 7, of which 6 were waited for; matrix products, arithmetic and copies ran while one was open for 11% of the time, Pallas kernels for 0%

commit v1 on v0

--- a/solution.py
+++ b/solution.py
@@ -7,6 +7,11 @@
 FSDP = ("fy", "fc")
 HEADS = 8
 HEAD_DIM = 96
+
+
+def swapped_in(x, axis, along):
+    sent = jnp.stack([x] * lax.axis_size(axis))
+    return jnp.concatenate(lax.all_to_all(sent, axis, 0, 0), axis=along)
 
 
 def split_heads(frames):
@@ -90,9 +95,7 @@
     context, soft_probs, rounded = attend(frames, segment)
     columns = context
     mixed_sums = jnp.dot(
-        columns,
-        lax.all_gather(out_weight, FSDP, axis=0, tiled=True),
-        preferred_element_type=jnp.float32,
+        columns, swapped_in(out_weight, FSDP, 0), preferred_element_type=jnp.float32
     )
     mixed = mixed_sums.astype(jnp.bfloat16)
     result, pullback = jax.vjp(

time: 212 us -> 269 us (1.27)
  blocking collectives: 20.6 us -> 51.5 us
  waiting for transfers between devices: 76.9 us -> 102 us
  local copies, waits for them, and re-layouts: 12.8 us -> 21.3 us
  starting transfers between devices: 46.4 us -> 37.9 us
    all_to_all x1, waiting for transfers between devices: 16 us -> 59.4 us  [swapped_in(): return jnp.concatenate(lax.all_to_all(sent, axis, 0, 0), axis=along)]
    all_to_all x0 -> x1, blocking collectives: none -> 31 us  [body(): lax.all_to_all(outgoing, DP, split_axis=0, concat_axis=0, tiled=True)]
    reduce_scatter x1, waiting for transfers between devices: 12.4 us -> 0.02 us  [body(): lax.psum_scatter(jnp.einsum('rc,rd->cd', columns, mixed_grad, preferred_e...]
    all_gather x1, waiting for transfers between devices: 11.6 us -> 0.02 us  [body(): lax.all_gather(out_weight, FSDP, axis=0, tiled=True)]
    reshape x31, local copies, waits for them, and re-layouts: 0.2 us -> 8.54 us  [finish(): kernel[offset] * padded[offset:offset + length] * matching[:, None]]
    all_to_all x1, starting transfers between devices: 10 us -> 5 us  [body(): lax.all_to_all(returning, DP, split_axis=0, concat_axis=0, tiled=True)]
    all_to_all x1, waiting for transfers between devices: 0.01 us -> 4.71 us  [sum_rows(): lax.all_to_all(padded.reshape(count, per, x.shape[1]), axis, split_axis=0...]
    all_to_all x1, starting transfers between devices: 13.7 us -> 9.71 us  [swapped_in(): return jnp.concatenate(lax.all_to_all(sent, axis, 0, 0), axis=along)]
  transfers between devices with their start and end apart: 7 -> 7, of which waited for: 6 -> 5; matrix products, arithmetic and copies ran while one was open for 11% -> 20% of each run, Pallas kernels for 0% -> 0%
where the time goes in v1:
time: 269 us; the launch traced here: 268 us
  waiting for transfers between devices  102 us (38%)
  blocking collectives  51.5 us (19%)
  starting transfers between devices  37.9 us (14%)
  other arithmetic  27.5 us (10%)
  local copies, waits for them, and re-layouts  21.3 us (8%)
  between operations  14.9 us (6%)
  matrix products  13.2 us (5%)
    all_to_all x1, waiting for transfers between devices, swapped_in(): return jnp.concatenate(lax.all_to_all(sent, axis, 0, 0), axis=along)  59.4 us
    all_to_all x1, blocking collectives, body(): lax.all_to_all(outgoing, DP, split_axis=0, concat_axis=0, tiled=True)  31 us
    all_to_all x1, blocking collectives, sum_rows(): lax.all_to_all(padded.reshape(count, per, x.shape[1]), axis, split_axis=0...  20.5 us
    all_to_all x2, starting transfers between devices, gather_rows(): got = lax.all_to_all(copies, axis, split_axis=0, concat_axis=0, tiled=True)  18.5 us
    all_to_all x2, waiting for transfers between devices, gather_rows(): got = lax.all_to_all(copies, axis, split_axis=0, concat_axis=0, tiled=True)  18.4 us
    all_to_all x1, waiting for transfers between devices, body(): lax.all_to_all(returning, DP, split_axis=0, concat_axis=0, tiled=True)  18.4 us
    reduce_sum x4, other arithmetic, finish(): kernel[offset] * padded[offset:offset + length] * matching[:, None]  15.2 us
    all_to_all x1, starting transfers between devices, swapped_in(): return jnp.concatenate(lax.all_to_all(sent, axis, 0, 0), axis=along)  9.71 us
  transfers between devices with their start and end apart: 7, of which 5 were waited for; matrix products, arithmetic and copies ran while one was open for 20% of the time, Pallas kernels for 0%

profile of v1, /device:TPU:1, one launch (start us, length us, event | category | flops | bytes accessed | tf_op | source)
XLA Modules:
  0.0 267.9 jit_solution(16116399148430500624)
XLA Ops:
  7.2 1.2 compare_select_fusion.1
  8.4 0.7 broadcast_compare_fusion.3
  9.1 1.0 gather_fusion
  10.4 31.0 %all_to_all.49 = bf16[32,4,2304]{2,1,0:T(4,128)(2,1)S(1)} all-to-all(bf16[32,4,2304]{2,1,0:T(4,128)(2,1)S(1)} %all_to_all.31), channel_id=1, replica_groups=mesh['dz'=8,'dx'=4,'fy'=8,'fc'=2] {'dz','dx'}, dimensions={0} | all-to-all | bytes 1179648 | tf_op jit(solution)/shard_map/all_to_all | solution.py:91
  41.4 1.7 stack.2
  43.1 9.7 %all-to-all-start.1 = ((bf16[16,48,1536]{2,1,0:T(8,128)(2,1)}), bf16[16,48,1536]{2,1,0:T(8,128)(2,1)}, u32[]{:S(2)}, u32[]{:S(2)}) async-start(bf16[16,48,1536]{2,1,0:T(8,128)(2,1)} %stack.2), calls=%async_computation.1 | async-start | bytes 4718592 | tf_op jit(solution)/shard_map/all_to_all | solution.py:14
  52.8 0.7 all-gather.2.cloned.1.call-update
  53.6 0.6 compare_select_fusion
  54.2 0.2 slice_reduce_fusion.29
  54.4 0.3 slice_reduce_fusion.30
  55.2 1.0 gather_fusion.1
  56.6 0.2 copy.47
  56.8 0.2 copy.45
  56.9 1.2 fusion.39
  58.1 0.5 convolution_convert_fusion.6
  58.6 59.4 %all-to-all-done.1 = bf16[16,48,1536]{2,1,0:T(8,128)(2,1)} async-done(((bf16[16,48,1536]{2,1,0:T(8,128)(2,1)}), bf16[16,48,1536]{2,1,0:T(8,128)(2,1)}, u32[]{:S(2)}, u32[]{:S(2)}) %all-to-all-start.1) | async-done | bytes 2359328 | tf_op jit(solution)/shard_map/all_to_all | solution.py:14
  118.0 2.2 fusion.2
  120.2 7.7 %multiply_reduce_fusion.31 = (f32[1536]{0:T(1024)}, f32[1536]{0:T(1024)}, f32[1536]{0:T(1024)}, f32[1536]{0:T(1024)}, f32[1536]{0:T(1024)}, /*index=5*/f32[1536]...) fusion(f32[128,1536]{1,0:T(8,128)S(1)} %fusion.2, ...), kind=kLoop, calls=%fused_computation.99 | loop fusion | flops 25152000 | bytes 3013632 | tf_op jit(solution)/shard_map/transpose(jvp())/reduce_sum | solution.py:81
  128.0 2.3 multiply_reduce_fusion.16
  130.2 2.6 multiply_reduce_fusion.4
  132.9 0.5 multiply_multiply_fusion.27
  133.4 0.7 multiply_multiply_fusion.28
  134.2 0.7 multiply_multiply_fusion.29
  134.9 2.6 pad_add_fusion
  137.6 0.7 fusion.16
  138.2 2.1 convolution_convert_fusion
  140.4 2.5 convolution_convert_fusion.5
  143.1 0.3 fusion.40
  143.5 1.6 convolution_convert_fusion.4
  145.2 2.6 multiply_reduce_fusion.22
  147.9 0.7 reshape.300
  148.6 0.7 reshape.304
  149.3 0.7 reshape.305
  150.1 0.7 reshape.306
  150.8 0.7 reshape.307
  151.5 0.7 reshape.308
  152.2 0.7 reshape.309
  152.9 0.7 reshape.310
  153.6 0.7 reshape.312
  154.3 0.7 reshape.313
  155.0 0.7 reshape.314
  155.7 0.7 reshape.315
  156.6 0.3 pad_add_fusion.7
  156.9 0.8 reshape.316
  157.7 4.6 %all-to-all-start.3 = ((f32[16,2,1536]{2,1,0:T(2,128)}), f32[16,2,1536]{2,1,0:T(2,128)S(1)}, u32[]{:S(2)}, u32[]{:S(2)}) async-start(f32[16,2,1536]{2,1,0:T(2,128)} %reshape.316), calls=%async_computation.4 | async-start | bytes 393216 | tf_op jit(solution)/shard_map/all_to_all | solution.py:148
  162.4 1.5 convolution_convert_fusion.3
  164.1 1.3 convolution_convert_fusion.2
  165.5 1.8 scatter_custom_fusion
  167.3 1.0 all_to_all.35
  168.2 4.7 %all-to-all-done.3 = f32[16,2,1536]{2,1,0:T(2,128)S(1)} async-done(((f32[16,2,1536]{2,1,0:T(2,128)}), f32[16,2,1536]{2,1,0:T(2,128)S(1)}, u32[]{:S(2)}, u32[]{:S(2)}) %all-to-all-start.3) | async-done | bytes 196640 | tf_op jit(solution)/shard_map/all_to_all | solution.py:148
  172.9 5.0 %all-to-all-start.2 = ((bf16[32,4,2304]{2,1,0:T(4,128)(2,1)}), bf16[32,4,2304]{2,1,0:T(4,128)(2,1)S(1)}, u32[]{:S(2)}, u32[]{:S(2)}) async-start(bf16[32,4,2304]{2,1,0:T(4,128)(2,1)} %all_to_all.35), calls=%async_computation.2 | async-start | bytes 1179648 | tf_op jit(solution)/shard_map/all_to_all | solution.py:124
  178.0 18.4 %all-to-all-done.2 = bf16[32,4,2304]{2,1,0:T(4,128)(2,1)S(1)} async-done(((bf16[32,4,2304]{2,1,0:T(4,128)(2,1)}), bf16[32,4,2304]{2,1,0:T(4,128)(2,1)S(1)}, u32[]{:S(2)}, u32[]{:S(2)}) %all-to-all-start.2) | async-done | bytes 589856 | tf_op jit(solution)/shard_map/all_to_all | solution.py:124
  196.5 0.9 convert_element_type.218
  197.5 0.2 reshape.317
  197.8 20.5 %all_to_all.50 = f32[32,2,1536]{2,1,0:T(2,128)S(1)} all-to-all(f32[32,2,1536]{2,1,0:T(2,128)S(1)} %reshape.317), channel_id=1, replica_groups=mesh['dz'=8,'dx'=4,'fy'=8,'fc'=2] {'dz','dx'}, dimensions={0} | all-to-all | bytes 786432 | tf_op jit(solution)/shard_map/all_to_all | solution.py:148
  218.4 0.8 broadcast_in_dim.55
  219.2 5.7 %all-to-all-start.5 = ((f32[32,2,1536]{2,1,0:T(2,128)}), f32[32,2,1536]{2,1,0:T(2,128)S(1)}, u32[]{:S(2)}, u32[]{:S(2)}) async-start(f32[32,2,1536]{2,1,0:T(2,128)} %broadcast_in_dim.55), calls=%async_computation.6 | async-start | bytes 786432 | tf_op jit(solution)/shard_map/all_to_all | solution.py:157
  224.9 2.4 scatter_custom_fusion.1
  227.3 9.1 %all-to-all-done.5 = f32[32,2,1536]{2,1,0:T(2,128)S(1)} async-done(((f32[32,2,1536]{2,1,0:T(2,128)}), f32[32,2,1536]{2,1,0:T(2,128)S(1)}, u32[]{:S(2)}, u32[]{:S(2)}) %all-to-all-start.5) | async-done | bytes 393248 | tf_op jit(solution)/shard_map/all_to_all | solution.py:157
  236.4 0.7 broadcast_in_dim.57
  237.1 12.8 %all-to-all-start.6 = ((f32[16,2,1536]{2,1,0:T(2,128)}), f32[16,2,1536]{2,1,0:T(2,128)S(1)}, u32[]{:S(2)}, u32[]{:S(2)}) async-start(f32[16,2,1536]{2,1,0:T(2,128)} %broadcast_in_dim.57), calls=%async_computation.7 | async-start | bytes 393216 | tf_op jit(solution)/shard_map/all_to_all | solution.py:157
  250.1 0.9 mul.1323
  251.0 9.3 %all-to-all-done.6 = f32[16,2,1536]{2,1,0:T(2,128)S(1)} async-done(((f32[16,2,1536]{2,1,0:T(2,128)}), f32[16,2,1536]{2,1,0:T(2,128)S(1)}, u32[]{:S(2)}, u32[]{:S(2)}) %all-to-all-start.6) | async-done | bytes 196640 | tf_op jit(solution)/shard_map/all_to_all | solution.py:157
  260.4 0.7 slice_multiply_fusion.1
  (104 shorter events, 2.7 us)
Async XLA Ops:
  7.2 1.9 copy-start
  10.1 31.3 %copy-start.2 = (bf16[48,1536]{1,0:T(8,128)(2,1)S(1)}, bf16[48,1536]{1,0:T(8,128)(2,1)}, u32[]{:S(2)}) copy-start(bf16[48,1536]{1,0:T(8,128)(2,1)} %param.10) | copy-start | bytes 442372
  43.1 10.5 %copy-start.25 = (s32[128]{0:T(128)S(1)}, s32[128]{0:T(128)}, u32[]{:S(2)}) copy-start(s32[128]{0:T(128)} %param.14) | copy-start | bytes 1540
  43.1 11.1 %copy-start.5 = (f32[31,1536]{1,0:T(8,128)S(1)}, f32[31,1536]{1,0:T(8,128)}, u32[]{:S(2)}) copy-start(f32[31,1536]{1,0:T(8,128)} %param.11) | copy-start | bytes 571396
  43.1 11.6 %copy-start.24 = (s32[128]{0:T(128)S(1)}, s32[128]{0:T(128)}, u32[]{:S(2)}) copy-start(s32[128]{0:T(128)} %param.15) | copy-start | bytes 1540
  43.1 75.0 %all-to-all-start.1 = ((bf16[16,48,1536]{2,1,0:T(8,128)(2,1)}), bf16[16,48,1536]{2,1,0:T(8,128)(2,1)}, u32[]{:S(2)}, u32[]{:S(2)}) async-start(bf16[16,48,1536]{2,1,0:T(8,128)(2,1)} %stack.2), calls=%async_computation.1 | async-start | bytes 4718592 | tf_op jit(solution)/shard_map/all_to_all | solution.py:14
  52.8 87.6 %all-gather.2.cloned.1.call-start = ((), (), s32[]{:S(2)}) async-start(), calls=%async_computation.8 | async-start | bytes 2506752 | tf_op jit(solution)/shard_map/all_gather | solution.py:117
  53.5 143.0 %reduce-scatter.2.cloned.1.call-start = ((), (), s32[]{:S(2)}) async-start(), calls=%async_computation.9 | async-start | bytes 2506752 | tf_op jit(solution)/shard_map/reduce_scatter | solution.py:106
  54.9 78.5 %copy-start.15 = (f32[128]{0:T(128)}, f32[128]{0:T(128)S(1)}, u32[]{:S(2)}) copy-start(f32[128]{0:T(128)S(1)} %get-tuple-element.116) | copy-start | bytes 1540
  54.9 78.5 %copy-start.16 = (f32[128]{0:T(128)}, f32[128]{0:T(128)S(1)}, u32[]{:S(2)}) copy-start(f32[128]{0:T(128)S(1)} %get-tuple-element.117) | copy-start | bytes 1540
  54.9 78.5 %copy-start.17 = (f32[128]{0:T(128)}, f32[128]{0:T(128)S(1)}, u32[]{:S(2)}) copy-start(f32[128]{0:T(128)S(1)} %get-tuple-element.118) | copy-start | bytes 1540
  54.9 78.5 %copy-start.18 = (f32[128]{0:T(128)}, f32[128]{0:T(128)S(1)}, u32[]{:S(2)}) copy-start(f32[128]{0:T(128)S(1)} %get-tuple-element.119) | copy-start | bytes 1540
  55.0 78.5 %copy-start.19 = (f32[128]{0:T(128)}, f32[128]{0:T(128)S(1)}, u32[]{:S(2)}) copy-start(f32[128]{0:T(128)S(1)} %get-tuple-element.120) | copy-start | bytes 1540
  55.0 78.5 %copy-start.20 = (f32[128]{0:T(128)}, f32[128]{0:T(128)S(1)}, u32[]{:S(2)}) copy-start(f32[128]{0:T(128)S(1)} %get-tuple-element.121) | copy-start | bytes 1540
  55.0 79.2 %copy-start.21 = (f32[128]{0:T(128)}, f32[128]{0:T(128)S(1)}, u32[]{:S(2)}) copy-start(f32[128]{0:T(128)S(1)} %get-tuple-element.122) | copy-start | bytes 1540
  55.0 79.2 %copy-start.22 = (f32[128]{0:T(128)}, f32[128]{0:T(128)S(1)}, u32[]{:S(2)}) copy-start(f32[128]{0:T(128)S(1)} %get-tuple-element.123) | copy-start | bytes 1540
  55.0 79.2 %copy-start.23 = (f32[128]{0:T(128)}, f32[128]{0:T(128)S(1)}, u32[]{:S(2)}) copy-start(f32[128]{0:T(128)S(1)} %get-tuple-element.124) | copy-start | bytes 1540
  55.1 3.0 %copy-start.14 = (pred[128,128]{0,1:T(8,128)(4,1)}, pred[128,128]{0,1:T(8,128)(4,1)S(1)}, u32[]{:S(2)}) copy-start(pred[128,128]{0,1:T(8,128)(4,1)S(1)} %broadcast_compare_fusion) | copy-start | bytes 49156
  56.8 61.3 %copy-start.3 = (bf16[128,768]{0,1:T(8,128)(2,1)}, bf16[128,768]{0,1:T(8,128)(2,1)S(1)}, u32[]{:S(2)}) copy-start(bf16[128,768]{0,1:T(8,128)(2,1)S(1)} %copy.47) | copy-start | bytes 589828
  58.1 62.1 %copy-start.26 = (f32[8,128]{1,0:T(8,128)}, f32[8,128]{1,0:T(8,128)S(1)}, u32[]{:S(2)}) copy-start(f32[8,128]{1,0:T(8,128)S(1)} %get-tuple-element.144) | copy-start | bytes 12292
  58.6 61.6 %copy-start.1 = (bf16[128,1536]{1,0:T(8,128)(2,1)S(1)}, bf16[128,1536]{1,0:T(8,128)(2,1)}, u32[]{:S(2)}) copy-start(bf16[128,1536]{1,0:T(8,128)(2,1)} %param.12) | copy-start | bytes 1179652
  143.4 10.2 %copy-start.13 = (f32[1536]{0:T(1024)S(1)}, f32[1536]{0:T(1024)}, u32[]{:S(2)}) copy-start(f32[1536]{0:T(1024)} %get-tuple-element.33) | copy-start | bytes 18436
  143.4 13.0 %copy-start.12 = (f32[1536]{0:T(1024)S(1)}, f32[1536]{0:T(1024)}, u32[]{:S(2)}) copy-start(f32[1536]{0:T(1024)} %get-tuple-element.7) | copy-start | bytes 18436
  143.4 13.0 %copy-start.11 = (f32[1536]{0:T(1024)S(1)}, f32[1536]{0:T(1024)}, u32[]{:S(2)}) copy-start(f32[1536]{0:T(1024)} %get-tuple-element.8) | copy-start | bytes 18436
  143.4 13.0 %copy-start.10 = (f32[1536]{0:T(1024)S(1)}, f32[1536]{0:T(1024)}, u32[]{:S(2)}) copy-start(f32[1536]{0:T(1024)} %get-tuple-element.9) | copy-start | bytes 18436
  143.5 13.0 %copy-start.9 = (f32[1536]{0:T(1024)S(1)}, f32[1536]{0:T(1024)}, u32[]{:S(2)}) copy-start(f32[1536]{0:T(1024)} %get-tuple-element.10) | copy-start | bytes 18436
  143.5 13.0 %copy-start.8 = (f32[1536]{0:T(1024)S(1)}, f32[1536]{0:T(1024)}, u32[]{:S(2)}) copy-start(f32[1536]{0:T(1024)} %get-tuple-element.11) | copy-start | bytes 18436
  143.5 13.0 %copy-start.7 = (f32[1536]{0:T(1024)S(1)}, f32[1536]{0:T(1024)}, u32[]{:S(2)}) copy-start(f32[1536]{0:T(1024)} %get-tuple-element.12) | copy-start | bytes 18436
  143.5 13.1 %copy-start.6 = (f32[1536]{0:T(1024)S(1)}, f32[1536]{0:T(1024)}, u32[]{:S(2)}) copy-start(f32[1536]{0:T(1024)} %get-tuple-element.13) | copy-start | bytes 18436
  156.4 7.6 %copy-start.4 = (bf16[128,768]{0,1:T(8,128)(2,1)S(1)}, bf16[128,768]{0,1:T(8,128)(2,1)}, u32[]{:S(2)}) copy-start(bf16[128,768]{0,1:T(8,128)(2,1)} %copy-done.3) | copy-start | bytes 589828
  156.4 7.6 %copy-start.27 = (f32[8,128]{1,0:T(8,128)S(1)}, f32[8,128]{1,0:T(8,128)}, u32[]{:S(2)}) copy-start(f32[8,128]{1,0:T(8,128)} %copy-done.26) | copy-start | bytes 12292
  157.7 15.2 %all-to-all-start.3 = ((f32[16,2,1536]{2,1,0:T(2,128)}), f32[16,2,1536]{2,1,0:T(2,128)S(1)}, u32[]{:S(2)}, u32[]{:S(2)}) async-start(f32[16,2,1536]{2,1,0:T(2,128)} %reshape.316), calls=%async_computation.4 | async-start | bytes 393216 | tf_op jit(solution)/shard_map/all_to_all | solution.py:148
  172.9 23.4 %all-to-all-start.2 = ((bf16[32,4,2304]{2,1,0:T(4,128)(2,1)}), bf16[32,4,2304]{2,1,0:T(4,128)(2,1)S(1)}, u32[]{:S(2)}, u32[]{:S(2)}) async-start(bf16[32,4,2304]{2,1,0:T(4,128)(2,1)} %all_to_all.35), calls=%async_computation.2 | async-start | bytes 1179648 | tf_op jit(solution)/shard_map/all_to_all | solution.py:124
  219.2 17.2 %all-to-all-start.5 = ((f32[32,2,1536]{2,1,0:T(2,128)}), f32[32,2,1536]{2,1,0:T(2,128)S(1)}, u32[]{:S(2)}, u32[]{:S(2)}) async-start(f32[32,2,1536]{2,1,0:T(2,128)} %broadcast_in_dim.55), calls=%async_computation.6 | async-start | bytes 786432 | tf_op jit(solution)/shard_map/all_to_all | solution.py:157
  237.1 23.1 %all-to-all-start.6 = ((f32[16,2,1536]{2,1,0:T(2,128)}), f32[16,2,1536]{2,1,0:T(2,128)S(1)}, u32[]{:S(2)}, u32[]{:S(2)}) async-start(f32[16,2,1536]{2,1,0:T(2,128)} %broadcast_in_dim.57), calls=%async_computation.7 | async-start | bytes 393216 | tf_op jit(solution)/shard_map/all_to_all | solution.py:157
Sparse Core Ops, SparseCore 0:
  55.7 64.0 all-gather.1
  140.5 54.9 reduce-scatter.1
